TPU v7x, 256 devices: a whole 4x4x8 slice. The times are simulated.
256 devices in a mesh: row: 8 (over z), col: 32 (over y, x, core).
Axes of the slice: x: 4, y: 4, z: 8, core: 2. Of those that a mesh axis runs over, the one named last changes fastest.
Arguments:
- tokens: bfloat16 [512, 8192], P('col', 'row'), may hold values from -6 to 6
- cotangent: bfloat16 [512, 8192], P('col', 'row'), may hold values from -6 to 6
- w_gate: bfloat16 [8192, 16384], P('row', 'col'), may hold values from -0.09375 to 0.09375
- w_up: bfloat16 [8192, 16384], P('row', 'col'), may hold values from -0.09375 to 0.09375
- w_down: bfloat16 [16384, 8192], P('col', 'row'), may hold values from -0.0625 to 0.0625
- order_gate: int32 [2048], replicated, may hold values from 0 to 2047, each once
- order_up: int32 [2048], replicated, may hold values from 0 to 2047, each once
- order_down: int32 [2048], replicated, may hold values from 0 to 2047, each once
Outputs:
- output: bfloat16 [512, 8192], P('col', 'row')
- input_grad: bfloat16 [512, 8192], P('col', 'row')
- gate_weight_grad: float32 [8192, 16384], P('row', 'col')
- up_weight_grad: float32 [8192, 16384], P('row', 'col')
- down_weight_grad: float32 [16384, 8192], P('col', 'row')
Inputs may be any that keep to these rules, and one draw needn't show every extreme that they name: `order_gate`: each of the 2048 block numbers appears exactly once. `order_up`: each of the 2048 block numbers appears exactly once. `order_down`: each of the 2048 block numbers appears exactly once.
All inputs are finite; a program needn't handle non-finite values.
Results may differ from a plain program's by a relative error of at most 0.0049.
Values may be sent and summed in bfloat16 or wider, within the bound.
No kernel may reach another device: no remote copies, remote signals or barrier semaphores. Data moves between devices by JAX's collectives and lax.ppermute only.
A program may use at most 64 MiB of HBM per device.

v0:
```python
import jax
import jax.numpy as jnp
from jax import lax
from jax.sharding import PartitionSpec as P

BLOCK = 256


def kept_table(order, row_first, col_first, row_count, col_count, stride):
    kept_count = order.shape[0] // 2
    row_ids = row_first + jnp.arange(row_count, dtype=jnp.int32)
    col_ids = col_first + jnp.arange(col_count, dtype=jnp.int32)
    block_ids = row_ids[:, None] * stride + col_ids[None, :]
    return jnp.any(block_ids[:, :, None] == order[:kept_count][None, None, :], axis=2)


def expand_mask(kept_mask):
    row_count, col_count = kept_mask.shape
    spread = jnp.broadcast_to(kept_mask[:, None, :, None], (row_count, BLOCK, col_count, BLOCK))
    return spread.reshape(row_count * BLOCK, col_count * BLOCK)


def dense_apply(left_operand, right_operand, kept_mask, product_kind):
    full_mask = expand_mask(kept_mask)
    if product_kind == "forward":
        masked = right_operand * full_mask.astype(right_operand.dtype)
        return jnp.dot(left_operand, masked, preferred_element_type=jnp.float32)
    if product_kind == "transposed":
        masked = right_operand * full_mask.astype(right_operand.dtype)
        return lax.dot_general(
            left_operand, masked, (((1,), (1,)), ((), ())), preferred_element_type=jnp.float32
        )
    product = lax.dot_general(
        left_operand, right_operand, (((0,), (0,)), ((), ())), preferred_element_type=jnp.float32
    )
    return product * full_mask.astype(jnp.float32)


def apply_blocks(left_operand, right_operand, kept_mask, product_kind):
    return dense_apply(left_operand, right_operand, kept_mask, product_kind)


def on_device(tokens, cotangent, w_gate, w_up, w_down, order_gate, order_up, order_down):
    rows_here = w_gate.shape[0] // BLOCK
    cols_here = w_gate.shape[1] // BLOCK
    row_start = lax.axis_index("row") * rows_here
    col_start = lax.axis_index("col") * cols_here
    width_blocks = rows_here * lax.axis_size("row")
    hidden_blocks = cols_here * lax.axis_size("col")
    keep_gate = kept_table(order_gate, row_start, col_start, rows_here, cols_here, hidden_blocks)
    keep_up = kept_table(order_up, row_start, col_start, rows_here, cols_here, hidden_blocks)
    keep_down = kept_table(order_down, col_start, row_start, cols_here, rows_here, width_blocks)
    tokens_all = lax.all_gather(tokens, "col", axis=0, tiled=True)
    gate_term = apply_blocks(tokens_all, w_gate, keep_gate, "forward")
    up_term = apply_blocks(tokens_all, w_up, keep_up, "forward")
    gate, up = (
        lax.psum_scatter(gate_term, "row", scatter_dimension=0, tiled=True),
        lax.psum_scatter(up_term, "row", scatter_dimension=0, tiled=True),
    )
    sigmoid_gate = jax.nn.sigmoid(gate)
    activation = gate * sigmoid_gate
    hidden = (activation * up).astype(jnp.bfloat16)
    hidden_all = lax.all_gather(hidden, "row", axis=0, tiled=True)
    output_term = apply_blocks(hidden_all, w_down, keep_down, "forward")
    output = lax.psum_scatter(output_term, "col", scatter_dimension=0, tiled=True).astype(
        jnp.bfloat16
    )
    cotangent_all = lax.all_gather(cotangent, "col", axis=0, tiled=True)
    hidden_term = apply_blocks(cotangent_all, w_down, keep_down, "transposed")
    hidden_grad = lax.psum_scatter(hidden_term, "row", scatter_dimension=0, tiled=True)
    gate_grad = (hidden_grad * up * sigmoid_gate * (1.0 + gate * (1.0 - sigmoid_gate))).astype(
        jnp.bfloat16
    )
    up_grad = (hidden_grad * activation).astype(jnp.bfloat16)
    gate_grad_all, up_grad_all = (
        lax.all_gather(gate_grad, "row", axis=0, tiled=True),
        lax.all_gather(up_grad, "row", axis=0, tiled=True),
    )
    down_weight_grad = apply_blocks(hidden_all, cotangent_all, keep_down, "weights")
    gate_weight_grad = apply_blocks(tokens_all, gate_grad_all, keep_gate, "weights")
    up_weight_grad = apply_blocks(tokens_all, up_grad_all, keep_up, "weights")
    through_gate = apply_blocks(gate_grad_all, w_gate, keep_gate, "transposed")
    through_up = apply_blocks(up_grad_all, w_up, keep_up, "transposed")
    gate_share = lax.psum_scatter(through_gate, "col", scatter_dimension=0, tiled=True)
    up_share = lax.psum_scatter(through_up, "col", scatter_dimension=0, tiled=True)
    input_grad = gate_share + up_share
    return (
        output,
        input_grad.astype(jnp.bfloat16),
        gate_weight_grad,
        up_weight_grad,
        down_weight_grad,
    )


def solution(mesh):
    placed = (
        P("col", "row"),
        P("col", "row"),
        P("row", "col"),
        P("row", "col"),
        P("col", "row"),
        P(),
        P(),
        P(),
    )
    return jax.shard_map(
        on_device,
        mesh=mesh,
        in_specs=placed,
        out_specs=(
            P("col", "row"),
            P("col", "row"),
            P("row", "col"),
            P("row", "col"),
            P("col", "row"),
        ),
        check_vma=False,
    )
```

profile of v0, /device:TPU:2, one launch (start us, length us, event | category | flops | bytes accessed | tf_op | source)
XLA Modules:
  0.0 445.8 jit_solution(2200922386354329133)
XLA Ops:
  7.2 0.7 all-gather.5.cloned.1.call-update
  7.9 0.7 all-gather.3.cloned.1.call-update
  8.7 0.7 slice.11
  10.3 50.4 %all-gather.5.cloned.1.call-done = bf16[512,1024]{1,0:T(8,128)(2,1)} async-done(((bf16[16,1024]{1,0:T(8,128)(2,1)}), bf16[512,1024]{1,0:T(8,128)(2,1)}) %all-gather.5.cloned.1.call-update) | async-done | bytes 1048592 | tf_op jit(solution)/shard_map/all_gather | solution.py:68
  60.8 2.3 convolution_bitcast_fusion
  63.1 1.3 copy.46
  65.9 44.4 %all-gather.3.cloned.1.call-done = bf16[512,1024]{1,0:T(8,128)(2,1)} async-done(((bf16[16,1024]{1,0:T(8,128)(2,1)}), bf16[512,1024]{1,0:T(8,128)(2,1)}) %all-gather.3.cloned.1.call-update) | async-done | bytes 1048592 | tf_op jit(solution)/shard_map/all_gather | solution.py:53
  110.3 2.0 convolution_bitcast_fusion.2
  112.3 1.3 copy.42
  114.3 1.7 copy.34
  116.0 2.9 convolution_bitcast_fusion.1
  118.9 2.5 copy.44
  121.6 30.7 %reduce-scatter.20.cloned.1.call-done = f32[64,512]{1,0:T(8,128)} async-done(((f32[512,512]{1,0:T(8,128)}), f32[64,512]{1,0:T(8,128)}) %reduce-scatter.20.cloned.1.call-update) | async-done | bytes 131088 | tf_op jit(solution)/shard_map/reduce_scatter | solution.py:70
  152.3 40.6 %reduce-scatter.16.cloned.1.call-done = f32[64,512]{1,0:T(8,128)} async-done(((f32[512,512]{1,0:T(8,128)}), f32[64,512]{1,0:T(8,128)}) %reduce-scatter.16.cloned.1.call-update) | async-done | bytes 131088 | tf_op jit(solution)/shard_map/reduce_scatter | solution.py:57
  192.9 40.0 %reduce-scatter.18.cloned.1.call-done = f32[64,512]{1,0:T(8,128)} async-done(((f32[512,512]{1,0:T(8,128)}), f32[64,512]{1,0:T(8,128)}) %reduce-scatter.18.cloned.1.call-update) | async-done | bytes 131088 | tf_op jit(solution)/shard_map/reduce_scatter | solution.py:58
  232.9 1.1 multiply_convert_fusion
  234.1 25.5 %all_gather.16 = bf16[512,512]{1,0:T(8,128)(2,1)S(1)} all-gather(bf16[64,512]{1,0:T(8,128)(2,1)S(1)} %get-tuple-element.29), channel_id=1, replica_groups=mesh['row'=8,'col'=32] {'row'}, dimensions={0}, use_global_device_ids=true | all-gather | bytes 589824 | tf_op jit(solution)/shard_map/all_gather | solution.py:63
  259.6 3.3 fusion.1
  262.9 25.5 %all_gather.18 = bf16[512,512]{1,0:T(8,128)(2,1)S(1)} all-gather(bf16[64,512]{1,0:T(8,128)(2,1)S(1)} %get-tuple-element.28), channel_id=1, replica_groups=mesh['row'=8,'col'=32] {'row'}, dimensions={0}, use_global_device_ids=true | all-gather | bytes 589824 | tf_op jit(solution)/shard_map/all_gather | solution.py:76
  288.4 25.2 %all_gather.19 = bf16[512,512]{1,0:T(8,128)(2,1)S(1)} all-gather(bf16[64,512]{1,0:T(8,128)(2,1)S(1)} %get-tuple-element.27), channel_id=1, replica_groups=mesh['row'=8,'col'=32] {'row'}, dimensions={0}, use_global_device_ids=true | all-gather | bytes 589824 | tf_op jit(solution)/shard_map/all_gather | solution.py:77
  313.7 2.0 fusion.9
  315.7 2.1 convolution_add_fusion
  317.8 1.0 copy-done.8
  319.1 2.0 bitcast_select_fusion.1
  321.2 3.0 copy.40
  324.2 2.1 bitcast_select_fusion
  326.2 3.0 copy.41
  329.2 2.0 convolution_select_fusion
  331.3 16.4 %reduce-scatter.12.cloned.1.call-done = f32[16,1024]{1,0:T(8,128)} async-done(((f32[512,1024]{1,0:T(8,128)}), f32[16,1024]{1,0:T(8,128)}) %reduce-scatter.12.cloned.1.call-update) | async-done | bytes 65552 | tf_op jit(solution)/shard_map/reduce_scatter | solution.py:65
  347.7 1.5 convert_element_type.11
  349.1 88.4 %reduce-scatter.14.cloned.1.call-done = f32[16,1024]{1,0:T(8,128)} async-done(((f32[512,1024]{1,0:T(8,128)}), f32[16,1024]{1,0:T(8,128)}) %reduce-scatter.14.cloned.1.call-update) | async-done | bytes 65552 | tf_op jit(solution)/shard_map/reduce_scatter | solution.py:84
  437.5 1.5 convert_element_type.28
  (52 shorter events, 3.7 us)
Async XLA Ops:
  7.2 53.6 %all-gather.5.cloned.1.call-start = ((), (), s32[]{:S(2)}) async-start(), calls=%async_computation.7 | async-start | bytes 1081344 | tf_op jit(solution)/shard_map/all_gather | solution.py:68
  7.9 102.4 %all-gather.3.cloned.1.call-start = ((), (), s32[]{:S(2)}) async-start(), calls=%async_computation.5 | async-start | bytes 1081344 | tf_op jit(solution)/shard_map/all_gather | solution.py:53
  8.6 143.6 %reduce-scatter.20.cloned.1.call-start = ((), (), s32[]{:S(2)}) async-start(), calls=%async_computation.11 | async-start | bytes 1179648 | tf_op jit(solution)/shard_map/reduce_scatter | solution.py:70
  10.3 249.3 %copy-start.5 = (pred[64,8,4,256]{3,1,2,0:T(8,128)(4,1)}, pred[64,8,4,256]{3,1,2,0:T(8,128)(4,1)S(1)}, u32[]{:S(2)}) copy-start(pred[64,8,4,256]{3,1,2,0:T(8,128)(4,1)S(1)} %copy.50) | copy-start | bytes 1572868
  63.0 1.5 slice-start
  63.1 1.5 slice-start.1
  63.1 2.3 copy-start.9
  64.4 128.5 %reduce-scatter.16.cloned.1.call-start = ((), (), s32[]{:S(2)}) async-start(), calls=%async_computation.9 | async-start | bytes 1179648 | tf_op jit(solution)/shard_map/reduce_scatter | solution.py:57
  65.4 46.9 %copy-start.7 = (pred[64,8,4,256]{3,1,2,0:T(8,128)(4,1)}, pred[64,8,4,256]{3,1,2,0:T(8,128)(4,1)S(1)}, u32[]{:S(2)}) copy-start(pred[64,8,4,256]{3,1,2,0:T(8,128)(4,1)S(1)} %copy.48) | copy-start | bytes 1572868
  113.6 119.3 %reduce-scatter.18.cloned.1.call-start = ((), (), s32[]{:S(2)}) async-start(), calls=%async_computation.10 | async-start | bytes 1179648 | tf_op jit(solution)/shard_map/reduce_scatter | solution.py:58
  114.3 4.6 %copy-start = (pred[64,8,4,256]{3,1,2,0:T(8,128)(4,1)}, pred[64,8,4,256]{3,1,2,0:T(8,128)(4,1)S(1)}, u32[]{:S(2)}) copy-start(pred[64,8,4,256]{3,1,2,0:T(8,128)(4,1)S(1)} %copy.49) | copy-start | bytes 1572868
  121.5 226.2 %reduce-scatter.12.cloned.1.call-start = ((), (), s32[]{:S(2)}) async-start(), calls=%async_computation.6 | async-start | bytes 2162688 | tf_op jit(solution)/shard_map/reduce_scatter | solution.py:65
  262.9 174.6 %reduce-scatter.14.cloned.1.call-start = ((), (), s32[]{:S(2)}) async-start(), calls=%async_computation.8 | async-start | bytes 2162688 | tf_op jit(solution)/shard_map/reduce_scatter | solution.py:84
  313.7 2.0 copy-start.3
  313.7 2.0 copy-start.1
  317.7 1.0 copy-start.8
  317.7 1.4 copy-start.11
  321.2 3.0 copy-start.2
  321.2 3.0 copy-start.4
  326.2 3.0 copy-start.6
  326.2 3.0 copy-start.10
Sparse Core Ops, SparseCore 0:
  10.5 50.1 all-gather.4
  63.3 46.9 all-gather.2
  113.4 38.7 reduce-scatter.19
  155.2 37.6 reduce-scatter.15
  195.3 37.6 reduce-scatter.17
  263.0 84.6 reduce-scatter.11
  351.5 85.9 reduce-scatter.13
where the time goes:
time: 446 us
  waiting for transfers between devices  312 us (70%)
  blocking collectives  76.2 us (17%)
  matrix products  20.7 us (5%)
  local copies, waits for them, and re-layouts  17.3 us (4%)
  between operations  14.3 us (3%)
  other arithmetic  4.62 us (1%)
    reduce_scatter x1, waiting for transfers between devices, on_device(): lax.psum_scatter(through_gate, 'col', scatter_dimension=0, tiled=True)  88.4 us
    all_gather x1, waiting for transfers between devices, on_device(): cotangent_all = lax.all_gather(cotangent, 'col', axis=0, tiled=True)  50.4 us
    all_gather x1, waiting for transfers between devices, on_device(): tokens_all = lax.all_gather(tokens, 'col', axis=0, tiled=True)  44.4 us
    reduce_scatter x1, waiting for transfers between devices, on_device(): lax.psum_scatter(gate_term, 'row', scatter_dimension=0, tiled=True)  40.6 us
    reduce_scatter x1, waiting for transfers between devices, on_device(): lax.psum_scatter(up_term, 'row', scatter_dimension=0, tiled=True)  40 us
    reduce_scatter x1, waiting for transfers between devices, on_device(): lax.psum_scatter(hidden_term, 'row', scatter_dimension=0, tiled=True)  30.7 us
    all_gather x1, blocking collectives, on_device(): hidden_all = lax.all_gather(hidden, 'row', axis=0, tiled=True)  25.5 us
    all_gather x1, blocking collectives, on_device(): lax.all_gather(gate_grad, 'row', axis=0, tiled=True)  25.5 us
  transfers between devices with their start and end apart: 7, of which 7 were waited for; matrix products, arithmetic and copies ran while one was open for 8% of the time, Pallas kernels for 0%

commit v1 on v0

--- a/solution.py
+++ b/solution.py
@@ -50,7 +50,8 @@
     keep_gate = kept_table(order_gate, row_start, col_start, rows_here, cols_here, hidden_blocks)
     keep_up = kept_table(order_up, row_start, col_start, rows_here, cols_here, hidden_blocks)
     keep_down = kept_table(order_down, col_start, row_start, cols_here, rows_here, width_blocks)
-    tokens_all = lax.all_gather(tokens, "col", axis=0, tiled=True)
+    outgoing = jnp.stack([tokens] * lax.axis_size("col"))
+    tokens_all = jnp.concatenate(lax.all_to_all(outgoing, "col", 0, 0), axis=0)
     gate_term = apply_blocks(tokens_all, w_gate, keep_gate, "forward")
     up_term = apply_blocks(tokens_all, w_up, keep_up, "forward")
     gate, up = (

time: 446 us -> 372 us (0.83)
  waiting for transfers between devices: 312 us -> 223 us
  starting transfers between devices: 0.28 us -> 8.06 us
    all_gather x1 -> x0, waiting for transfers between devices: 44.4 us -> none  [on_device(): tokens_all = lax.all_gather(tokens, 'col', axis=0, tiled=True)]
    all_gather x1, waiting for transfers between devices: 50.4 us -> 16.8 us  [on_device(): cotangent_all = lax.all_gather(cotangent, 'col', axis=0, tiled=True)]
    reduce_scatter x1, waiting for transfers between devices: 40.6 us -> 7.82 us  [on_device(): lax.psum_scatter(gate_term, 'row', scatter_dimension=0, tiled=True)]
    all_to_all x0 -> x1, waiting for transfers between devices: none -> 14.7 us  [on_device(): tokens_all = jnp.concatenate(lax.all_to_all(outgoing, 'col', 0, 0), axis=0)]
    reduce_scatter x1, waiting for transfers between devices: 30.7 us -> 40.6 us  [on_device(): lax.psum_scatter(hidden_term, 'row', scatter_dimension=0, tiled=True)]
    all_to_all x0 -> x1, starting transfers between devices: none -> 7.8 us  [on_device(): tokens_all = jnp.concatenate(lax.all_to_all(outgoing, 'col', 0, 0), axis=0)]
    unnamed x34 -> x32, local copies, waits for them, and re-layouts: 15.5 us -> 16.4 us
  transfers between devices with their start and end apart: 7 -> 7, of which waited for: 7 -> 7; matrix products, arithmetic and copies ran while one was open for 8% -> 11% of each run, Pallas kernels for 0% -> 0%
where the time goes in v1:
time: 372 us; the launch traced here: 371 us
  waiting for transfers between devices  223 us (60%)
  blocking collectives  76.2 us (20%)
  matrix products  24.1 us (6%)
  local copies, waits for them, and re-layouts  19.3 us (5%)
  between operations  15.6 us (4%)
  starting transfers between devices  8.06 us (2%)
  other arithmetic  4.62 us (1%)
    reduce_scatter x1, waiting for transfers between devices, on_device(): lax.psum_scatter(through_gate, 'col', scatter_dimension=0, tiled=True)  88.4 us
    reduce_scatter x1, waiting for transfers between devices, on_device(): lax.psum_scatter(hidden_term, 'row', scatter_dimension=0, tiled=True)  40.6 us
    reduce_scatter x1, waiting for transfers between devices, on_device(): lax.psum_scatter(up_term, 'row', scatter_dimension=0, tiled=True)  39.9 us
    all_gather x1, blocking collectives, on_device(): lax.all_gather(gate_grad, 'row', axis=0, tiled=True)  25.7 us
    all_gather x1, blocking collectives, on_device(): hidden_all = lax.all_gather(hidden, 'row', axis=0, tiled=True)  25.4 us
    all_gather x1, blocking collectives, on_device(): lax.all_gather(up_grad, 'row', axis=0, tiled=True)  25.2 us
    all_gather x1, waiting for transfers between devices, on_device(): cotangent_all = lax.all_gather(cotangent, 'col', axis=0, tiled=True)  16.8 us
    unnamed x32, local copies, waits for them, and re-layouts  16.4 us
  transfers between devices with their start and end apart: 7, of which 7 were waited for; matrix products, arithmetic and copies ran while one was open for 11% of the time, Pallas kernels for 0%

profile of v1, /device:TPU:2, one launch (start us, length us, event | category | flops | bytes accessed | tf_op | source)
XLA Modules:
  0.0 371.4 jit_solution(10322259020676261030)
XLA Ops:
  8.1 0.7 all-gather.2.cloned.1.call-update
  8.8 1.9 stack.2
  10.6 7.8 %all-to-all-start = ((bf16[32,16,1024]{2,1,0:T(8,128)(2,1)}), bf16[32,16,1024]{2,1,0:T(8,128)(2,1)}, u32[]{:S(2)}, u32[]{:S(2)}) async-start(bf16[32,16,1024]{2,1,0:T(8,128)(2,1)} %stack.2), calls=%async_computation | async-start | bytes 2097152 | tf_op jit(solution)/shard_map/all_to_all | solution.py:54
  20.0 14.7 %all-to-all-done = bf16[32,16,1024]{2,1,0:T(8,128)(2,1)} async-done(((bf16[32,16,1024]{2,1,0:T(8,128)(2,1)}), bf16[32,16,1024]{2,1,0:T(8,128)(2,1)}, u32[]{:S(2)}, u32[]{:S(2)}) %all-to-all-start) | async-done | bytes 1048608 | tf_op jit(solution)/shard_map/all_to_all | solution.py:54
  34.7 2.0 convolution_bitcast_fusion.2
  36.7 1.3 copy.42
  38.7 1.7 copy.34
  40.3 2.9 convolution_bitcast_fusion.1
  43.3 2.6 copy.44
  46.9 16.8 %all-gather.2.cloned.1.call-done = bf16[512,1024]{1,0:T(8,128)(2,1)} async-done(((bf16[16,1024]{1,0:T(8,128)(2,1)}), bf16[512,1024]{1,0:T(8,128)(2,1)}) %all-gather.2.cloned.1.call-update) | async-done | bytes 1048592 | tf_op jit(solution)/shard_map/all_gather | solution.py:69
  63.7 3.3 convolution_bitcast_fusion
  66.9 2.5 copy.46
  69.5 7.8 %reduce-scatter.16.cloned.1.call-done = f32[64,512]{1,0:T(8,128)} async-done(((f32[512,512]{1,0:T(8,128)}), f32[64,512]{1,0:T(8,128)}) %reduce-scatter.16.cloned.1.call-update) | async-done | bytes 131088 | tf_op jit(solution)/shard_map/reduce_scatter | solution.py:58
  77.4 39.9 %reduce-scatter.18.cloned.1.call-done = f32[64,512]{1,0:T(8,128)} async-done(((f32[512,512]{1,0:T(8,128)}), f32[64,512]{1,0:T(8,128)}) %reduce-scatter.18.cloned.1.call-update) | async-done | bytes 131088 | tf_op jit(solution)/shard_map/reduce_scatter | solution.py:59
  117.3 40.6 %reduce-scatter.20.cloned.1.call-done = f32[64,512]{1,0:T(8,128)} async-done(((f32[512,512]{1,0:T(8,128)}), f32[64,512]{1,0:T(8,128)}) %reduce-scatter.20.cloned.1.call-update) | async-done | bytes 131088 | tf_op jit(solution)/shard_map/reduce_scatter | solution.py:71
  157.9 1.1 multiply_convert_fusion
  159.0 25.4 %all_gather.12 = bf16[512,512]{1,0:T(8,128)(2,1)S(1)} all-gather(bf16[64,512]{1,0:T(8,128)(2,1)S(1)} %get-tuple-element.29), channel_id=1, replica_groups=mesh['row'=8,'col'=32] {'row'}, dimensions={0}, use_global_device_ids=true | all-gather | bytes 589824 | tf_op jit(solution)/shard_map/all_gather | solution.py:64
  184.3 3.3 fusion.1
  187.7 25.7 %all_gather.14 = bf16[512,512]{1,0:T(8,128)(2,1)S(1)} all-gather(bf16[64,512]{1,0:T(8,128)(2,1)S(1)} %get-tuple-element.28), channel_id=1, replica_groups=mesh['row'=8,'col'=32] {'row'}, dimensions={0}, use_global_device_ids=true | all-gather | bytes 589824 | tf_op jit(solution)/shard_map/all_gather | solution.py:77
  213.4 25.2 %all_gather.15 = bf16[512,512]{1,0:T(8,128)(2,1)S(1)} all-gather(bf16[64,512]{1,0:T(8,128)(2,1)S(1)} %get-tuple-element.27), channel_id=1, replica_groups=mesh['row'=8,'col'=32] {'row'}, dimensions={0}, use_global_device_ids=true | all-gather | bytes 589824 | tf_op jit(solution)/shard_map/all_gather | solution.py:78
  238.6 2.0 fusion.9
  240.6 2.1 convolution_add_fusion
  242.7 1.0 copy-done.6
  243.7 3.3 bitcast_select_fusion.1
  247.0 3.0 copy.40
  250.0 3.3 bitcast_select_fusion
  253.2 3.0 copy.41
  256.2 2.0 convolution_select_fusion
  258.3 14.5 %reduce-scatter.12.cloned.1.call-done = f32[16,1024]{1,0:T(8,128)} async-done(((f32[512,1024]{1,0:T(8,128)}), f32[16,1024]{1,0:T(8,128)}) %reduce-scatter.12.cloned.1.call-update) | async-done | bytes 65552 | tf_op jit(solution)/shard_map/reduce_scatter | solution.py:66
  272.8 1.5 convert_element_type.11
  274.2 88.4 %reduce-scatter.14.cloned.1.call-done = f32[16,1024]{1,0:T(8,128)} async-done(((f32[512,1024]{1,0:T(8,128)}), f32[16,1024]{1,0:T(8,128)}) %reduce-scatter.14.cloned.1.call-update) | async-done | bytes 65552 | tf_op jit(solution)/shard_map/reduce_scatter | solution.py:85
  362.6 1.5 convert_element_type.28
  (51 shorter events, 3.3 us)
Async XLA Ops:
  8.0 10.6 %slice-start = ((s32[2048]{0:T(1024)}), s32[1024]{0:T(1024)S(1)}, s32[]{:S(2)}) async-start(s32[2048]{0:T(1024)} %param.13), calls=%async_computation.12 | async-start | bytes 8192 | tf_op jit(solution)/shard_map/slice | solution.py:14
  8.0 10.6 %slice-start.1 = ((s32[2048]{0:T(1024)}), s32[1024]{0:T(1024)S(1)}, s32[]{:S(2)}) async-start(s32[2048]{0:T(1024)} %param.14), calls=%async_computation.13 | async-start | bytes 8192 | tf_op jit(solution)/shard_map/slice | solution.py:14
  8.0 55.7 %all-gather.2.cloned.1.call-start = ((), (), s32[]{:S(2)}) async-start(), calls=%async_computation.7 | async-start | bytes 1081344 | tf_op jit(solution)/shard_map/all_gather | solution.py:69
  10.6 8.8 %copy-start.9 = (bf16[1024,512]{1,0:T(8,128)(2,1)S(1)}, bf16[1024,512]{1,0:T(8,128)(2,1)}, u32[]{:S(2)}) copy-start(bf16[1024,512]{1,0:T(8,128)(2,1)} %param.10) | copy-start | bytes 3145732
  10.6 24.1 %all-to-all-start = ((bf16[32,16,1024]{2,1,0:T(8,128)(2,1)}), bf16[32,16,1024]{2,1,0:T(8,128)(2,1)}, u32[]{:S(2)}, u32[]{:S(2)}) async-start(bf16[32,16,1024]{2,1,0:T(8,128)(2,1)} %stack.2), calls=%async_computation | async-start | bytes 2097152 | tf_op jit(solution)/shard_map/all_to_all | solution.py:54
  18.4 58.9 %reduce-scatter.16.cloned.1.call-start = ((), (), s32[]{:S(2)}) async-start(), calls=%async_computation.9 | async-start | bytes 1179648 | tf_op jit(solution)/shard_map/reduce_scatter | solution.py:58
  19.4 17.2 %copy-start.5 = (pred[64,8,4,256]{3,1,2,0:T(8,128)(4,1)}, pred[64,8,4,256]{3,1,2,0:T(8,128)(4,1)S(1)}, u32[]{:S(2)}) copy-start(pred[64,8,4,256]{3,1,2,0:T(8,128)(4,1)S(1)} %copy.48) | copy-start | bytes 1572868
  38.0 79.3 %reduce-scatter.18.cloned.1.call-start = ((), (), s32[]{:S(2)}) async-start(), calls=%async_computation.10 | async-start | bytes 1179648 | tf_op jit(solution)/shard_map/reduce_scatter | solution.py:59
  38.7 4.6 %copy-start = (pred[64,8,4,256]{3,1,2,0:T(8,128)(4,1)}, pred[64,8,4,256]{3,1,2,0:T(8,128)(4,1)S(1)}, u32[]{:S(2)}) copy-start(pred[64,8,4,256]{3,1,2,0:T(8,128)(4,1)S(1)} %copy.49) | copy-start | bytes 1572868
  43.3 2.7 slice-start.2
  45.9 112.0 %reduce-scatter.20.cloned.1.call-start = ((), (), s32[]{:S(2)}) async-start(), calls=%async_computation.11 | async-start | bytes 1179648 | tf_op jit(solution)/shard_map/reduce_scatter | solution.py:71
  46.8 137.5 %copy-start.7 = (pred[64,8,4,256]{3,1,2,0:T(8,128)(4,1)}, pred[64,8,4,256]{3,1,2,0:T(8,128)(4,1)S(1)}, u32[]{:S(2)}) copy-start(pred[64,8,4,256]{3,1,2,0:T(8,128)(4,1)S(1)} %copy.50) | copy-start | bytes 1572868
  69.5 203.3 %reduce-scatter.12.cloned.1.call-start = ((), (), s32[]{:S(2)}) async-start(), calls=%async_computation.6 | async-start | bytes 2162688 | tf_op jit(solution)/shard_map/reduce_scatter | solution.py:66
  187.7 175.0 %reduce-scatter.14.cloned.1.call-start = ((), (), s32[]{:S(2)}) async-start(), calls=%async_computation.8 | async-start | bytes 2162688 | tf_op jit(solution)/shard_map/reduce_scatter | solution.py:85
  238.6 2.0 copy-start.3
  238.6 2.0 copy-start.1
  242.7 1.0 copy-start.6
  247.0 3.0 copy-start.2
  247.0 3.0 copy-start.4
  253.2 3.0 copy-start.8
  253.2 3.0 copy-start.10
Sparse Core Ops, SparseCore 0:
  11.4 52.2 all-gather.1
  187.8 84.9 reduce-scatter.11
  276.6 85.9 reduce-scatter.13
Sparse Core Ops, SparseCore 1:
  38.1 39.2 reduce-scatter.15
  79.8 37.4 reduce-scatter.17
  120.2 37.6 reduce-scatter.19
